TPU v7x, 128 devices: a whole 4x4x4 slice. The times are simulated.
128 devices in a mesh: section: 16 (over y, z_lo, core), sp: 8 (over z_hi, x).
Axes of the slice: x: 4, y: 4, z: 4 (z_hi: 2, z_lo: 2; z = z_hi * 2 + z_lo), core: 2. Of those that a mesh axis runs over, the one named last changes fastest.
Arguments:
- resid: float32 [16, 896, 6144], P('section', 'sp'), may hold values from -1.8 to 1.8
- qkv: bfloat16 [16, 896, 3, 6144], P('section', 'sp'), may hold values from -48 to 48
- cache_kv: bfloat16 [16, 2, 2, 1344, 6144], P('section', None, None, None, 'sp'), may hold values from -6 to 6
- out_proj: bfloat16 [16, 6144, 6144], P('section', 'sp'), may hold values from -0.078125 to 0.078125
- gate: float32 [16, 2, 6144], P('section'), may hold values from 0.5 to 2
- span_ids: int32 [16], P('section'), may hold values from 3 to 39
- cache_counts: int32 [16], P('section'), may hold values from 0 to 3, as said below
- span_mask: int32 [40, 40], replicated, may hold values from 0 to 1, as said below
Outputs:
- carried: float32 [16, 896, 6144], P('section', 'sp')
Inputs may be any that keep to these rules, and one draw needn't show every extreme that they name: `cache_counts`: some section has all 3 slots filled. span_mask[i][j] is 0 for j > i and 1 for j = i.
All inputs are finite; a program needn't handle non-finite values.
Results may differ from a plain program's by a relative error of at most 0.006.
Values may be sent and summed in bfloat16 or wider, within the bound.
No kernel may reach another device: no remote copies, remote signals or barrier semaphores. Data moves between devices by JAX's collectives and lax.ppermute only.
A program may use at most 384 MiB of HBM per device.

v0:
```python
import jax
import jax.numpy as jnp
from jax import lax
from jax.sharding import PartitionSpec as P

HDIM = 128
SPAN = 448
NCHUNK = 40
SLOTS = 3
VIDS = 2
TOKS = 896
KEYS = 1344


def passed_along(shard, axis, by):
    devices = lax.axis_size(axis)
    return lax.ppermute(shard, axis, [(i, (i + by) % devices) for i in range(devices)])


def visible_slots(span_id, filled, span_mask):
    row_mask = lax.dynamic_index_in_dim(span_mask, span_id, 0, keepdims=False)
    slot_ids = jnp.arange(SLOTS, dtype=jnp.int32)
    wanted = span_id - 1 - slot_ids
    columns = jnp.arange(NCHUNK, dtype=jnp.int32)
    looked = jnp.sum(jnp.where(columns[None, :] == wanted[:, None], row_mask[None, :], 0), axis=1)
    return (slot_ids < filled) & (looked == 1)


def far_scores(queries, cache_keys, live_slots):
    score_scale = HDIM ** (-0.5)
    scores = (
        jnp.einsum("qhe,khe->hqk", queries, cache_keys, preferred_element_type=jnp.float32)
        * score_scale
    )
    key_live = jnp.repeat(live_slots, SPAN)
    result = jnp.where(key_live[None, None, :], scores, -jnp.inf)
    return result


def mix_video(far_part, queries, own_keys, own_values, cache_values):
    score_scale = HDIM ** (-0.5)
    near_part = (
        jnp.einsum("qhe,khe->hqk", queries, own_keys, preferred_element_type=jnp.float32)
        * score_scale
    )
    scores = jnp.concatenate([far_part, near_part], axis=2)
    highest = jnp.max(scores, axis=2, keepdims=True)
    raised = jnp.exp(scores - highest)
    weights = (raised / jnp.sum(raised, axis=2, keepdims=True)).astype(jnp.bfloat16)
    values_all = jnp.concatenate([cache_values, own_values], axis=0)
    mixed = jnp.einsum("hqk,khe->qhe", weights, values_all, preferred_element_type=jnp.float32)
    return mixed.astype(jnp.bfloat16).reshape(SPAN, queries.shape[1] * HDIM)


def per_device(resid, qkv, cache_kv, out_proj, gate, span_ids, cache_counts, span_mask):
    own_rows = resid.shape[1]
    local_width = cache_kv.shape[4]
    local_heads = local_width // HDIM
    filled = cache_counts[0]
    live_slots = visible_slots(span_ids[0], filled, span_mask)
    cache_keys = cache_kv[0, 0].reshape(VIDS, KEYS, local_heads, HDIM)
    cache_values = cache_kv[0, 1].reshape(VIDS, KEYS, local_heads, HDIM)

    def score_video(inputs_one):
        return far_scores(inputs_one[0], inputs_one[1], live_slots)

    spread = lax.all_to_all(qkv[0], "sp", split_axis=2, concat_axis=0, tiled=True)
    queries = spread[:, 0].reshape(VIDS, SPAN, local_heads, HDIM)
    far_all = lax.map(score_video, (queries, cache_keys))
    own_keys = spread[:, 1].reshape(VIDS, SPAN, local_heads, HDIM)
    own_values = spread[:, 2].reshape(VIDS, SPAN, local_heads, HDIM)

    def mix_one(inputs_one):
        return mix_video(inputs_one[0], inputs_one[1], inputs_one[2], inputs_one[3], inputs_one[4])

    heads_all = lax.map(mix_one, (far_all, queries, own_keys, own_values, cache_values)).reshape(
        TOKS, local_width
    )
    partial = jnp.dot(heads_all, out_proj[0], preferred_element_type=jnp.float32)
    devices = lax.axis_size("sp")
    shares = partial.astype(jnp.bfloat16).reshape(devices, own_rows, partial.shape[1])
    shares = lax.all_to_all(shares, "sp", 0, 0, tiled=True)
    projected = jnp.sum(shares.astype(jnp.float32), axis=0)
    device_place = lax.axis_index("sp")
    video_of = (device_place * own_rows + jnp.arange(own_rows, dtype=jnp.int32)) // SPAN
    picker = (video_of[:, None] == jnp.arange(VIDS, dtype=jnp.int32)[None, :]).astype(jnp.float32)
    gains = jnp.dot(picker, gate[0], precision=lax.Precision.HIGHEST)
    layer_out = resid[0] + gains * projected
    return passed_along(layer_out[None], "section", 1)


def solution(mesh):
    in_specs = (
        P("section", "sp", None),
        P("section", "sp", None, None),
        P("section", None, None, None, "sp"),
        P("section", "sp", None),
        P("section", None, None),
        P("section"),
        P("section"),
        P(),
    )
    out_specs = P("section", "sp", None)
    return jax.shard_map(
        per_device, mesh=mesh, in_specs=in_specs, out_specs=out_specs, check_vma=False
    )
```

profile of v0, /device:TPU:6, one launch (start us, length us, event | category | flops | bytes accessed | tf_op | source)
XLA Modules:
  0.0 466.9 jit_solution(14958061917673568924)
XLA Ops:
  0.0 10.0 %copy.53 = bf16[1,112,3,6144]{1,2,3,0:T(4,128)(2,1)} copy(bf16[1,112,3,6144]{3,1,2,0:T(8,128)(2,1)} %param.13) | data formatting | bytes 8257536 | tf_op args[1]
  10.0 8.1 %all-to-all-start = ((bf16[112,3,6144]{0,1,2:T(4,128)(2,1)}), bf16[112,3,6144]{0,1,2:T(4,128)(2,1)}, u32[]{:S(2)}, u32[]{:S(2)}) async-start(bf16[112,3,6144]{0,1,2:T(4,128)(2,1)} %bitcast.82), calls=%async_computation | async-start | bytes 12582912 | tf_op jit(solution)/shard_map/all_to_all | solution.py:67
  19.4 5.7 %fusion.30 = (bf16[1,1,2,1344,768]{4,3,2,1,0:T(8,128)(2,1)}, bf16[1,1,2,1344,768]{4,3,2,1,0:T(8,128)(2,1)}) fusion(bf16[1,2,2,1344,768]{4,3,2,1,0:T(8,128)(2,1)} %param.14), kind=kLoop, calls=%fused_computation.45 | loop fusion | bytes 16515072 | tf_op jit(solution)/shard_map/slice | solution.py:61
  25.1 6.4 %copy.58 = bf16[1,1,2,1344,768]{3,4,2,1,0:T(8,128)(2,1)} copy(bf16[1,1,2,1344,768]{4,3,2,1,0:T(8,128)(2,1)} %get-tuple-element.147) | data formatting | bytes 8257536 | tf_op jit(solution)/shard_map/slice | solution.py:61
  31.5 6.4 %copy.60 = bf16[2,1344,6,128]{3,1,2,0:T(8,128)(2,1)} copy(bf16[2,1344,6,128]{1,3,2,0:T(8,128)(2,1)} %bitcast.83) | data formatting | bytes 8257536 | tf_op jit(solution)/shard_map/while | solution.py:69
  38.0 6.4 %copy.52 = bf16[1,1,2,1344,768]{3,4,2,1,0:T(8,128)(2,1)} copy(bf16[1,1,2,1344,768]{4,3,2,1,0:T(8,128)(2,1)} %get-tuple-element.148) | data formatting | bytes 8257536 | tf_op jit(solution)/shard_map/slice | solution.py:62
  44.4 6.4 %copy.62 = bf16[2,1344,6,128]{3,1,2,0:T(8,128)(2,1)} copy(bf16[2,1344,6,128]{1,3,2,0:T(8,128)(2,1)} %bitcast.84) | data formatting | bytes 8257536 | tf_op jit(solution)/shard_map/while | solution.py:76
  50.8 0.7 dynamic-slice_bitcast_fusion.3
  51.5 0.2 select_reduce_fusion
  51.7 59.1 %all-to-all-done = bf16[112,3,6144]{0,1,2:T(4,128)(2,1)} async-done(((bf16[112,3,6144]{0,1,2:T(4,128)(2,1)}), bf16[112,3,6144]{0,1,2:T(4,128)(2,1)}, u32[]{:S(2)}, u32[]{:S(2)}) %all-to-all-start) | async-done | bytes 4128800 | tf_op jit(solution)/shard_map/all_to_all | solution.py:67
  110.8 10.0 %copy.68 = bf16[112,3,8,768]{3,0,2,1:T(8,128)(2,1)} copy(bf16[112,3,8,768]{0,1,3,2:T(4,128)(2,1)} %bitcast.14) | data formatting | bytes 8257536 | tf_op jit(solution)/shard_map/all_to_all | solution.py:67
  120.8 3.5 fusion.31
  124.3 2.5 reshape.36
  126.8 1.7 copy.59
  128.5 18.3 %while.20 = (s32[]{:T(128)}, f32[2,6,448,1344]{3,2,1,0:T(8,128)}, pred[3]{0:T(512)(128)(4,1)S(1)}, bf16[2,448,6,128]{3,1,2,0:T(8,128)(2,1)S(1)}, bf16[2,1344,6,128]{3,1,2,0:T(8,128)(2,1)}, /*index=5*/s32[]{:T(128)}) while((s32[]{:T(128)}, f32[2,6,448,1344]{3,2,1,0:T(8,128)}, pred[3]{0:T(512)(128)(4,1)S(1)}, ...), condition=%wide.region_2.3_spmd, body=%wide.region_1.2_spmd.sunk | while | flops 932069376 | bytes 17899016 | solution.py:69
  128.7 8.9 %bitcast_dynamic-update-slice_fusion.2 = f32[2,6,448,1344]{3,2,1,0:T(8,128)} fusion(f32[2,6,448,1344]{3,2,1,0:T(8,128)} %get-tuple-element.241, s32[]{:T(128)} %get-tuple-element.240, pred[1344]{0:T(1024)(128)(4,1)S(1)} %broadcast_in_dim.72, bf16[2,1344,6,128]{3,1,2,0:T(8,128)(2,1)} %get-tuple-element.250, ...), kind=kOutput, calls=%fused_computation.clone.1 | convolution fusion | flops 932069376 | bytes 17894912 | tf_op jit(solution)/shard_map/while/body/eval_jaxpr/qhe,khe->hqk/dot_general | solution.py:32
  137.8 9.0 %bitcast_dynamic-update-slice_fusion.2 = f32[2,6,448,1344]{3,2,1,0:T(8,128)} fusion(f32[2,6,448,1344]{3,2,1,0:T(8,128)} %get-tuple-element.241, s32[]{:T(128)} %get-tuple-element.240, pred[1344]{0:T(1024)(128)(4,1)S(1)} %broadcast_in_dim.72, bf16[2,1344,6,128]{3,1,2,0:T(8,128)(2,1)} %get-tuple-element.250, ...), kind=kOutput, calls=%fused_computation.clone.1 | convolution fusion | flops 932069376 | bytes 17894912 | tf_op jit(solution)/shard_map/while/body/eval_jaxpr/qhe,khe->hqk/dot_general | solution.py:32
  146.8 4.1 reshape.34
  151.0 2.8 copy.63
  153.8 2.5 reshape.35
  156.3 2.8 copy.65
  159.1 81.1 %while.21 = (s32[]{:T(128)}, bf16[2,448,768]{2,1,0:T(8,128)(2,1)}, bf16[2,1344,6,128]{3,1,2,0:T(8,128)(2,1)}, bf16[2,448,6,128]{3,1,2,0:T(8,128)(2,1)}, f32[2,6,...) while((s32[]{:T(128)}, bf16[2,448,768]{2,1,0:T(8,128)(2,1)}, ...), condition=%wide.region_7.8_spmd, body=%wide.region_3.7_spmd.sunk | while | flops 1586989824 | bytes 108822680 | solution.py:76
  159.1 4.4 fusion.42
  163.5 11.6 %dynamic-slice_reduce_fusion.2 = (f32[6,448]{1,0:T(8,128)S(1)}, f32[6,448,1344]{2,1,0:T(8,128)}) fusion(f32[2,6,448,1344]{3,2,1,0:T(8,128)} %get-tuple-element.272, s32[]{:T(128)} %get-tuple-element.260), kind=kLoop, calls=%fused_computation.9.clone.1 | loop fusion | flops 3609984 | bytes 28912132 | tf_op jit(solution)/shard_map/while/body/eval_jaxpr/reduce_max | solution.py:47
  175.1 10.8 %fusion.43 = f32[6,448]{1,0:T(8,128)S(1)} fusion(f32[6,448,448]{2,1,0:T(8,128)} %get-tuple-element.230, f32[6,448,1344]{2,1,0:T(8,128)} %get-tuple-element.231, f32[6,448]{1,0:T(8,128)S(1)} %reduce_max.27), kind=kLoop, calls=%fused_computation.11.clone.1 | loop fusion | flops 14448000 | bytes 19289088 | tf_op jit(solution)/shard_map/while/body/eval_jaxpr/reduce_sum | solution.py:49
  185.9 0.1 dynamic-slice_bitcast_fusion.7
  186.1 1.2 copy-done.2
  187.2 0.9 dynamic-slice_bitcast_fusion.6
  188.1 10.0 %fusion.44 = bf16[448,6,128]{2,0,1:T(8,128)(2,1)S(1)} fusion(bf16[448,6,128]{2,0,1:T(8,128)(2,1)} %dynamic-slice_bitcast_fusion.6, bf16[1344,6,128]{2,0,1:T(8,128)(2,1)S(1)} %dynamic-slice_bitcast_fusion.7, f32[6,448,448]{2,1,0:T(8,128)} %get-tuple-element.230, f32[6,448,1344]{2,1,0:T(8,128)} %get-tuple-element.231, f32[6,448]{1,0:T(8,128)S(1)} %fusion.43, ...), kind=kOutput, calls=%fused_computation.19.clone.1 | convolution fusion | flops 1258242048 | bytes 22729728 | tf_op jit(solution)/shard_map/while/body/eval_jaxpr/hqk,khe->qhe/dot_general | solution.py:51
  198.2 0.3 copy.79
  198.4 0.3 copy.80
  198.7 0.9 constant_dynamic-update-slice_fusion.2
  199.6 4.4 fusion.42
  204.0 11.6 %dynamic-slice_reduce_fusion.2 = (f32[6,448]{1,0:T(8,128)S(1)}, f32[6,448,1344]{2,1,0:T(8,128)}) fusion(f32[2,6,448,1344]{3,2,1,0:T(8,128)} %get-tuple-element.272, s32[]{:T(128)} %get-tuple-element.260), kind=kLoop, calls=%fused_computation.9.clone.1 | loop fusion | flops 3609984 | bytes 28912132 | tf_op jit(solution)/shard_map/while/body/eval_jaxpr/reduce_max | solution.py:47
  215.6 10.8 %fusion.43 = f32[6,448]{1,0:T(8,128)S(1)} fusion(f32[6,448,448]{2,1,0:T(8,128)} %get-tuple-element.230, f32[6,448,1344]{2,1,0:T(8,128)} %get-tuple-element.231, f32[6,448]{1,0:T(8,128)S(1)} %reduce_max.27), kind=kLoop, calls=%fused_computation.11.clone.1 | loop fusion | flops 14448000 | bytes 19289088 | tf_op jit(solution)/shard_map/while/body/eval_jaxpr/reduce_sum | solution.py:49
  226.6 1.2 copy-done.2
  227.8 0.9 dynamic-slice_bitcast_fusion.6
  228.6 10.0 %fusion.44 = bf16[448,6,128]{2,0,1:T(8,128)(2,1)S(1)} fusion(bf16[448,6,128]{2,0,1:T(8,128)(2,1)} %dynamic-slice_bitcast_fusion.6, bf16[1344,6,128]{2,0,1:T(8,128)(2,1)S(1)} %dynamic-slice_bitcast_fusion.7, f32[6,448,448]{2,1,0:T(8,128)} %get-tuple-element.230, f32[6,448,1344]{2,1,0:T(8,128)} %get-tuple-element.231, f32[6,448]{1,0:T(8,128)S(1)} %fusion.43, ...), kind=kOutput, calls=%fused_computation.19.clone.1 | convolution fusion | flops 1258242048 | bytes 22729728 | tf_op jit(solution)/shard_map/while/body/eval_jaxpr/hqk,khe->qhe/dot_general | solution.py:51
  238.7 0.3 copy.79
  239.0 0.3 copy.80
  239.2 0.9 constant_dynamic-update-slice_fusion.2
  240.1 15.2 %convolution_convert_fusion = bf16[896,6144]{1,0:T(8,128)(2,1)} fusion(bf16[896,768]{1,0:T(8,128)(2,1)} %bitcast.87, bf16[1,768,6144]{2,1,0:T(8,128)(2,1)} %param.15), kind=kOutput, calls=%fused_computation.30 | convolution fusion | flops 8461221888 | bytes 21823488 | tf_op jit(solution)/shard_map/dot_general | solution.py:79
  255.4 6.9 %all-to-all-start.1 = ((bf16[8,112,6144]{2,1,0:T(8,128)(2,1)}), bf16[8,112,6144]{2,1,0:T(8,128)(2,1)}, u32[]{:S(2)}, u32[]{:S(2)}) async-start(bf16[8,112,6144]{2,1,0:T(8,128)(2,1)} %bitcast.86), calls=%async_computation.1 | async-start | bytes 22020096 | tf_op jit(solution)/shard_map/all_to_all | solution.py:82
  262.3 160.4 %all-to-all-done.1 = bf16[8,112,6144]{2,1,0:T(8,128)(2,1)} async-done(((bf16[8,112,6144]{2,1,0:T(8,128)(2,1)}), bf16[8,112,6144]{2,1,0:T(8,128)(2,1)}, u32[]{:S(2)}, u32[]{:S(2)}) %all-to-all-start.1) | async-done | bytes 11010080 | tf_op jit(solution)/shard_map/all_to_all | solution.py:82
  422.7 6.4 %convert_reduce_fusion = f32[112,6144]{1,0:T(8,128)S(1)} fusion(bf16[8,112,6144]{2,1,0:T(8,128)(2,1)} %all-to-all-done.1), kind=kLoop, calls=%fused_computation.29 | loop fusion | flops 10321920 | bytes 13762560 | tf_op jit(solution)/shard_map/reduce_sum | solution.py:83
  429.1 1.6 fusion.26
  430.8 34.6 %collective-permute-done = f32[1,112,6144]{2,1,0:T(8,128)S(1)} collective-permute-done((f32[1,112,6144]{2,1,0:T(8,128)S(1)}, f32[1,112,6144]{2,1,0:T(8,128)S(1)}, u32[]{:S(2)}, u32[]{:S(2)}) %collective-permute-start) | collective-permute-done | bytes 2752544 | tf_op jit(solution)/shard_map/ppermute | solution.py:17
  465.4 1.5 copy.100
  (23 shorter events, 0.6 us)
Async XLA Ops:
  0.0 429.1 %copy-start = (f32[1,2,6144]{2,1,0:T(2,128)S(1)}, f32[1,2,6144]{2,1,0:T(2,128)}, u32[]{:S(2)}) copy-start(f32[1,2,6144]{2,1,0:T(2,128)} %param.16) | copy-start | bytes 147460
  10.0 100.8 %all-to-all-start = ((bf16[112,3,6144]{0,1,2:T(4,128)(2,1)}), bf16[112,3,6144]{0,1,2:T(4,128)(2,1)}, u32[]{:S(2)}, u32[]{:S(2)}) async-start(bf16[112,3,6144]{0,1,2:T(4,128)(2,1)} %bitcast.82), calls=%async_computation | async-start | bytes 12582912 | tf_op jit(solution)/shard_map/all_to_all | solution.py:67
  175.1 10.8 %copy-start.1 = (bf16[2,1344,6,128]{3,1,2,0:T(8,128)(2,1)S(1)}, bf16[2,1344,6,128]{3,1,2,0:T(8,128)(2,1)}, u32[]{:S(2)}) copy-start(bf16[2,1344,6,128]{3,1,2,0:T(8,128)(2,1)} %get-tuple-element.270) | copy-start | bytes 12386308 | tf_op jit(solution)/shard_map/while
  185.9 1.3 copy-start.2
  215.6 10.8 %copy-start.1 = (bf16[2,1344,6,128]{3,1,2,0:T(8,128)(2,1)S(1)}, bf16[2,1344,6,128]{3,1,2,0:T(8,128)(2,1)}, u32[]{:S(2)}) copy-start(bf16[2,1344,6,128]{3,1,2,0:T(8,128)(2,1)} %get-tuple-element.270) | copy-start | bytes 12386308 | tf_op jit(solution)/shard_map/while
  226.4 1.3 copy-start.2
  255.4 167.3 %all-to-all-start.1 = ((bf16[8,112,6144]{2,1,0:T(8,128)(2,1)}), bf16[8,112,6144]{2,1,0:T(8,128)(2,1)}, u32[]{:S(2)}, u32[]{:S(2)}) async-start(bf16[8,112,6144]{2,1,0:T(8,128)(2,1)} %bitcast.86), calls=%async_computation.1 | async-start | bytes 22020096 | tf_op jit(solution)/shard_map/all_to_all | solution.py:82
  262.3 166.8 %copy-start.3 = (f32[1,112,6144]{2,1,0:T(8,128)S(1)}, f32[1,112,6144]{2,1,0:T(8,128)}, u32[]{:S(2)}) copy-start(f32[1,112,6144]{2,1,0:T(8,128)} %param.12) | copy-start | bytes 8257540
  430.7 34.7 %collective-permute-start = (f32[1,112,6144]{2,1,0:T(8,128)S(1)}, f32[1,112,6144]{2,1,0:T(8,128)S(1)}, u32[]{:S(2)}, u32[]{:S(2)}) collective-permute-start(f32[1,112,6144]{2,1,0:T(8,128)S(1)} %fusion.26), channel_id=1, source_target_pairs={{0,8},{8,16},{16,24},{24,32},{32,40},{40,48},{48,56},{56,64},{64,7... | collective-permute-start | bytes 8257544 | tf_op jit(solution)/shard_map/ppermute | solution.py:17
where the time goes:
time: 469 us; the launch traced here: 467 us
  waiting for transfers between devices  254 us (54%)
  local copies, waits for them, and re-layouts  81.3 us (17%)
  matrix products  63.6 us (14%)
  other arithmetic  51.5 us (11%)
  starting transfers between devices  15.1 us (3%)
    all_to_all x1, waiting for transfers between devices, per_device(): shares = lax.all_to_all(shares, 'sp', 0, 0, tiled=True)  160 us
    all_to_all x1, waiting for transfers between devices, per_device(): lax.all_to_all(qkv[0], 'sp', split_axis=2, concat_axis=0, tiled=True)  59.1 us
    ppermute x1, waiting for transfers between devices, passed_along(): lax.ppermute(shard, axis, [(i, (i + by) % devices) for i in range(devices)])  34.6 us
    reduce_max x4, other arithmetic, mix_video(): highest = jnp.max(scores, axis=2, keepdims=True)  23.2 us
    reduce_sum x2, other arithmetic, mix_video(): jnp.sum(raised, axis=2, keepdims=True)  21.6 us
    dot_general x2, matrix products, mix_video(): jnp.einsum('hqk,khe->qhe', weights, values_all, preferred_element_type=jn...  20.1 us
    dot_general x2, matrix products, far_scores(): jnp.einsum('qhe,khe->hqk', queries, cache_keys, preferred_element_type=jn...  18 us
    dot_general x1, matrix products, per_device(): jnp.dot(heads_all, out_proj[0], preferred_element_type=jnp.float32)  15.2 us
  transfers between devices with their start and end apart: 3, of which 3 were waited for; matrix products, arithmetic and copies ran while one was open for 7% of the time, Pallas kernels for 0%

commit v1 on v0

--- a/solution.py
+++ b/solution.py
@@ -1,3 +1,4 @@
+import functools
 import jax
 import jax.numpy as jnp
 from jax import lax
@@ -10,6 +11,22 @@
 VIDS = 2
 TOKS = 896
 KEYS = 1344
+
+
+def tables_derive(payload, ax_name):
+    top = jnp.concatenate(
+        lax.all_to_all(
+            jnp.stack(jnp.split(payload, lax.axis_size(ax_name), axis=2), axis=0),
+            axis_name=ax_name,
+            split_axis=0,
+            concat_axis=0,
+        ),
+        axis=0,
+    )
+    return top
+
+
+cut_stops_all = functools.partial(tables_derive, ax_name="sp")
 
 
 def passed_along(shard, axis, by):
@@ -64,7 +81,7 @@
     def score_video(inputs_one):
         return far_scores(inputs_one[0], inputs_one[1], live_slots)
 
-    spread = lax.all_to_all(qkv[0], "sp", split_axis=2, concat_axis=0, tiled=True)
+    spread = cut_stops_all(qkv[0])
     queries = spread[:, 0].reshape(VIDS, SPAN, local_heads, HDIM)
     far_all = lax.map(score_video, (queries, cache_keys))
     own_keys = spread[:, 1].reshape(VIDS, SPAN, local_heads, HDIM)

time: 469 us -> 427 us (0.910)
  waiting for transfers between devices: 254 us -> 222 us
  local copies, waits for them, and re-layouts: 81.3 us -> 72.6 us
    all_to_all x1, waiting for transfers between devices: 59.1 us -> 26.5 us  [tables_derive(): lax.all_to_all(jnp.stack(jnp.split(payload, lax.axis_size(ax_name), axis=...]
    all_to_all x1, local copies, waits for them, and re-layouts: 10 us -> 2.52 us  [tables_derive(): lax.all_to_all(jnp.stack(jnp.split(payload, lax.axis_size(ax_name), axis=...]
    unnamed x6 -> x14, local copies, waits for them, and re-layouts: 11.6 us -> 11.7 us
  transfers between devices with their start and end apart: 3 -> 3, of which waited for: 3 -> 3; matrix products, arithmetic and copies ran while one was open for 7% -> 8% of each run, Pallas kernels for 0% -> 0%
where the time goes in v1:
time: 427 us; the launch traced here: 426 us
  waiting for transfers between devices  222 us (52%)
  local copies, waits for them, and re-layouts  72.6 us (17%)
  matrix products  63.6 us (15%)
  other arithmetic  51.5 us (12%)
  starting transfers between devices  15.1 us (4%)
    all_to_all x1, waiting for transfers between devices, per_device(): shares = lax.all_to_all(shares, 'sp', 0, 0, tiled=True)  160 us
    ppermute x1, waiting for transfers between devices, passed_along(): lax.ppermute(shard, axis, [(i, (i + by) % devices) for i in range(devices)])  34.6 us
    all_to_all x1, waiting for transfers between devices, tables_derive(): lax.all_to_all(jnp.stack(jnp.split(payload, lax.axis_size(ax_name), axis=...  26.5 us
    reduce_max x4, other arithmetic, mix_video(): highest = jnp.max(scores, axis=2, keepdims=True)  23.2 us
    reduce_sum x2, other arithmetic, mix_video(): jnp.sum(raised, axis=2, keepdims=True)  21.6 us
    dot_general x2, matrix products, mix_video(): jnp.einsum('hqk,khe->qhe', weights, values_all, preferred_element_type=jn...  20.1 us
    dot_general x2, matrix products, far_scores(): jnp.einsum('qhe,khe->hqk', queries, cache_keys, preferred_element_type=jn...  18 us
    dot_general x1, matrix products, per_device(): jnp.dot(heads_all, out_proj[0], preferred_element_type=jnp.float32)  15.2 us
  transfers between devices with their start and end apart: 3, of which 3 were waited for; matrix products, arithmetic and copies ran while one was open for 8% of the time, Pallas kernels for 0%

profile of v1, /device:TPU:6, one launch (start us, length us, event | category | flops | bytes accessed | tf_op | source)
XLA Modules:
  0.0 425.9 jit_solution(6030224219934321928)
XLA Ops:
  0.0 2.0 fusion.34
  2.0 1.8 fusion.33
  3.9 1.9 fusion.32
  5.8 1.9 fusion.31
  7.6 0.9 fusion.30
  8.5 0.9 fusion.29
  9.4 0.8 fusion.28
  10.2 0.8 fusion.27
  11.0 8.1 %all-to-all-start = ((bf16[8,112,3,768]{3,1,2,0:T(8,128)(2,1)}), bf16[8,112,3,768]{3,1,2,0:T(8,128)(2,1)}, u32[]{:S(2)}, u32[]{:S(2)}) async-start(bf16[8,112,3,768]{3,1,2,0:T(8,128)(2,1)} %fusion.27), calls=%async_computation | async-start | bytes 8257536 | tf_op jit(solution)/shard_map/all_to_all | solution.py:18
  20.4 5.7 %fusion.38 = (bf16[1,1,2,1344,768]{4,3,2,1,0:T(8,128)(2,1)}, bf16[1,1,2,1344,768]{4,3,2,1,0:T(8,128)(2,1)}) fusion(bf16[1,2,2,1344,768]{4,3,2,1,0:T(8,128)(2,1)} %param.14), kind=kLoop, calls=%fused_computation.61 | loop fusion | bytes 16515072 | tf_op jit(solution)/shard_map/slice | solution.py:78
  26.1 6.5 %copy.67 = bf16[1,1,2,1344,768]{3,4,2,1,0:T(8,128)(2,1)} copy(bf16[1,1,2,1344,768]{4,3,2,1,0:T(8,128)(2,1)} %get-tuple-element.147) | data formatting | bytes 8257536 | tf_op jit(solution)/shard_map/slice | solution.py:78
  32.5 6.5 %copy.69 = bf16[2,1344,6,128]{3,1,2,0:T(8,128)(2,1)} copy(bf16[2,1344,6,128]{1,3,2,0:T(8,128)(2,1)} %bitcast.110) | data formatting | bytes 8257536 | tf_op jit(solution)/shard_map/while | solution.py:86
  39.0 6.5 %copy.63 = bf16[1,1,2,1344,768]{3,4,2,1,0:T(8,128)(2,1)} copy(bf16[1,1,2,1344,768]{4,3,2,1,0:T(8,128)(2,1)} %get-tuple-element.148) | data formatting | bytes 8257536 | tf_op jit(solution)/shard_map/slice | solution.py:79
  45.5 6.4 %copy.71 = bf16[2,1344,6,128]{3,1,2,0:T(8,128)(2,1)} copy(bf16[2,1344,6,128]{1,3,2,0:T(8,128)(2,1)} %bitcast.111) | data formatting | bytes 8257536 | tf_op jit(solution)/shard_map/while | solution.py:93
  52.8 26.5 %all-to-all-done = bf16[8,112,3,768]{3,1,2,0:T(8,128)(2,1)} async-done(((bf16[8,112,3,768]{3,1,2,0:T(8,128)(2,1)}), bf16[8,112,3,768]{3,1,2,0:T(8,128)(2,1)}, u32[]{:S(2)}, u32[]{:S(2)}) %all-to-all-start) | async-done | bytes 4128800 | tf_op jit(solution)/shard_map/all_to_all | solution.py:18
  79.4 2.5 copy.64
  81.9 1.3 fusion.39
  83.2 2.5 reshape.40
  85.7 1.7 copy.68
  87.4 18.4 %while.20 = (s32[]{:T(128)}, f32[2,6,448,1344]{3,2,1,0:T(8,128)}, pred[3]{0:T(512)(128)(4,1)S(1)}, bf16[2,448,6,128]{3,1,2,0:T(8,128)(2,1)S(1)}, bf16[2,1344,6,128]{3,1,2,0:T(8,128)(2,1)}, /*index=5*/s32[]{:T(128)}) while((s32[]{:T(128)}, f32[2,6,448,1344]{3,2,1,0:T(8,128)}, pred[3]{0:T(512)(128)(4,1)S(1)}, ...), condition=%wide.region_2.3_spmd, body=%wide.region_1.2_spmd.sunk | while | flops 932069376 | bytes 17899016 | solution.py:86
  87.6 9.0 %bitcast_dynamic-update-slice_fusion.2 = f32[2,6,448,1344]{3,2,1,0:T(8,128)} fusion(f32[2,6,448,1344]{3,2,1,0:T(8,128)} %get-tuple-element.241, s32[]{:T(128)} %get-tuple-element.240, pred[1344]{0:T(1024)(128)(4,1)S(1)} %broadcast_in_dim.72, bf16[2,1344,6,128]{3,1,2,0:T(8,128)(2,1)} %get-tuple-element.250, ...), kind=kOutput, calls=%fused_computation.clone.1 | convolution fusion | flops 932069376 | bytes 17894912 | tf_op jit(solution)/shard_map/while/body/eval_jaxpr/qhe,khe->hqk/dot_general | solution.py:49
  96.7 9.0 %bitcast_dynamic-update-slice_fusion.2 = f32[2,6,448,1344]{3,2,1,0:T(8,128)} fusion(f32[2,6,448,1344]{3,2,1,0:T(8,128)} %get-tuple-element.241, s32[]{:T(128)} %get-tuple-element.240, pred[1344]{0:T(1024)(128)(4,1)S(1)} %broadcast_in_dim.72, bf16[2,1344,6,128]{3,1,2,0:T(8,128)(2,1)} %get-tuple-element.250, ...), kind=kOutput, calls=%fused_computation.clone.1 | convolution fusion | flops 932069376 | bytes 17894912 | tf_op jit(solution)/shard_map/while/body/eval_jaxpr/qhe,khe->hqk/dot_general | solution.py:49
  105.8 4.1 reshape.38
  109.9 2.8 copy.72
  112.7 2.5 reshape.39
  115.2 2.8 copy.74
  118.0 81.0 %while.21 = (s32[]{:T(128)}, bf16[2,448,768]{2,1,0:T(8,128)(2,1)}, bf16[2,1344,6,128]{3,1,2,0:T(8,128)(2,1)}, bf16[2,448,6,128]{3,1,2,0:T(8,128)(2,1)}, f32[2,6,...) while((s32[]{:T(128)}, bf16[2,448,768]{2,1,0:T(8,128)(2,1)}, ...), condition=%wide.region_7.8_spmd, body=%wide.region_3.7_spmd.sunk | while | flops 1586989824 | bytes 108822680 | solution.py:93
  118.0 4.4 %fusion.50 = (f32[6,448]{1,0:T(8,128)S(1)}, f32[6,448,448]{2,1,0:T(8,128)}) fusion(bf16[2,448,6,128]{3,1,2,0:T(8,128)(2,1)} %get-tuple-element.274, s32[]{:T(128)} %get-tuple-element.260, bf16[2,448,6,128]{3,1,2,0:T(8,128)(2,1)S(1)} %get-tuple-element.273), kind=kOutput, calls=%fused_computation.60.clone.1 | convolution fusion | flops 310687104 | bytes 6204928 | tf_op jit(solution)/shard_map/while/body/eval_jaxpr/qhe,khe->hqk/dot_general | solution.py:60
  122.4 11.6 %dynamic-slice_reduce_fusion.2 = (f32[6,448]{1,0:T(8,128)S(1)}, f32[6,448,1344]{2,1,0:T(8,128)}) fusion(f32[2,6,448,1344]{3,2,1,0:T(8,128)} %get-tuple-element.272, s32[]{:T(128)} %get-tuple-element.260), kind=kLoop, calls=%fused_computation.9.clone.1 | loop fusion | flops 3609984 | bytes 28912132 | tf_op jit(solution)/shard_map/while/body/eval_jaxpr/reduce_max | solution.py:64
  134.0 10.8 %fusion.51 = f32[6,448]{1,0:T(8,128)S(1)} fusion(f32[6,448,448]{2,1,0:T(8,128)} %get-tuple-element.230, f32[6,448,1344]{2,1,0:T(8,128)} %get-tuple-element.231, f32[6,448]{1,0:T(8,128)S(1)} %reduce_max.27), kind=kLoop, calls=%fused_computation.11.clone.1 | loop fusion | flops 14448000 | bytes 19289088 | tf_op jit(solution)/shard_map/while/body/eval_jaxpr/reduce_sum | solution.py:66
  145.0 1.2 copy-done.2
  146.1 0.9 dynamic-slice_bitcast_fusion.6
  147.0 10.0 %fusion.52 = bf16[448,6,128]{2,0,1:T(8,128)(2,1)S(1)} fusion(bf16[448,6,128]{2,0,1:T(8,128)(2,1)} %dynamic-slice_bitcast_fusion.6, bf16[1344,6,128]{2,0,1:T(8,128)(2,1)S(1)} %dynamic-slice_bitcast_fusion.7, f32[6,448,448]{2,1,0:T(8,128)} %get-tuple-element.230, f32[6,448,1344]{2,1,0:T(8,128)} %get-tuple-element.231, f32[6,448]{1,0:T(8,128)S(1)} %fusion.51, ...), kind=kOutput, calls=%fused_computation.19.clone.1 | convolution fusion | flops 1258242048 | bytes 22729728 | tf_op jit(solution)/shard_map/while/body/eval_jaxpr/hqk,khe->qhe/dot_general | solution.py:68
  157.6 0.9 constant_dynamic-update-slice_fusion.2
  158.5 4.4 %fusion.50 = (f32[6,448]{1,0:T(8,128)S(1)}, f32[6,448,448]{2,1,0:T(8,128)}) fusion(bf16[2,448,6,128]{3,1,2,0:T(8,128)(2,1)} %get-tuple-element.274, s32[]{:T(128)} %get-tuple-element.260, bf16[2,448,6,128]{3,1,2,0:T(8,128)(2,1)S(1)} %get-tuple-element.273), kind=kOutput, calls=%fused_computation.60.clone.1 | convolution fusion | flops 310687104 | bytes 6204928 | tf_op jit(solution)/shard_map/while/body/eval_jaxpr/qhe,khe->hqk/dot_general | solution.py:60
  162.9 11.6 %dynamic-slice_reduce_fusion.2 = (f32[6,448]{1,0:T(8,128)S(1)}, f32[6,448,1344]{2,1,0:T(8,128)}) fusion(f32[2,6,448,1344]{3,2,1,0:T(8,128)} %get-tuple-element.272, s32[]{:T(128)} %get-tuple-element.260), kind=kLoop, calls=%fused_computation.9.clone.1 | loop fusion | flops 3609984 | bytes 28912132 | tf_op jit(solution)/shard_map/while/body/eval_jaxpr/reduce_max | solution.py:64
  174.5 10.8 %fusion.51 = f32[6,448]{1,0:T(8,128)S(1)} fusion(f32[6,448,448]{2,1,0:T(8,128)} %get-tuple-element.230, f32[6,448,1344]{2,1,0:T(8,128)} %get-tuple-element.231, f32[6,448]{1,0:T(8,128)S(1)} %reduce_max.27), kind=kLoop, calls=%fused_computation.11.clone.1 | loop fusion | flops 14448000 | bytes 19289088 | tf_op jit(solution)/shard_map/while/body/eval_jaxpr/reduce_sum | solution.py:66
  185.5 1.2 copy-done.2
  186.7 0.9 dynamic-slice_bitcast_fusion.6
  187.5 10.0 %fusion.52 = bf16[448,6,128]{2,0,1:T(8,128)(2,1)S(1)} fusion(bf16[448,6,128]{2,0,1:T(8,128)(2,1)} %dynamic-slice_bitcast_fusion.6, bf16[1344,6,128]{2,0,1:T(8,128)(2,1)S(1)} %dynamic-slice_bitcast_fusion.7, f32[6,448,448]{2,1,0:T(8,128)} %get-tuple-element.230, f32[6,448,1344]{2,1,0:T(8,128)} %get-tuple-element.231, f32[6,448]{1,0:T(8,128)S(1)} %fusion.51, ...), kind=kOutput, calls=%fused_computation.19.clone.1 | convolution fusion | flops 1258242048 | bytes 22729728 | tf_op jit(solution)/shard_map/while/body/eval_jaxpr/hqk,khe->qhe/dot_general | solution.py:68
  198.1 0.9 constant_dynamic-update-slice_fusion.2
  199.0 15.2 %convolution_convert_fusion = bf16[896,6144]{1,0:T(8,128)(2,1)} fusion(bf16[896,768]{1,0:T(8,128)(2,1)} %bitcast.122, bf16[1,768,6144]{2,1,0:T(8,128)(2,1)} %param.15), kind=kOutput, calls=%fused_computation.30 | convolution fusion | flops 8461221888 | bytes 21823488 | tf_op jit(solution)/shard_map/dot_general | solution.py:96
  214.3 6.9 %all-to-all-start.1 = ((bf16[8,112,6144]{2,1,0:T(8,128)(2,1)}), bf16[8,112,6144]{2,1,0:T(8,128)(2,1)}, u32[]{:S(2)}, u32[]{:S(2)}) async-start(bf16[8,112,6144]{2,1,0:T(8,128)(2,1)} %bitcast.113), calls=%async_computation.1 | async-start | bytes 22020096 | tf_op jit(solution)/shard_map/all_to_all | solution.py:99
  221.2 160.4 %all-to-all-done.1 = bf16[8,112,6144]{2,1,0:T(8,128)(2,1)} async-done(((bf16[8,112,6144]{2,1,0:T(8,128)(2,1)}), bf16[8,112,6144]{2,1,0:T(8,128)(2,1)}, u32[]{:S(2)}, u32[]{:S(2)}) %all-to-all-start.1) | async-done | bytes 11010080 | tf_op jit(solution)/shard_map/all_to_all | solution.py:99
  381.6 6.4 %convert_reduce_fusion = f32[112,6144]{1,0:T(8,128)S(1)} fusion(bf16[8,112,6144]{2,1,0:T(8,128)(2,1)} %all-to-all-done.1), kind=kLoop, calls=%fused_computation.29 | loop fusion | flops 10321920 | bytes 13762560 | tf_op jit(solution)/shard_map/reduce_sum | solution.py:100
  388.1 1.6 fusion.26
  389.7 34.6 %collective-permute-done = f32[1,112,6144]{2,1,0:T(8,128)S(1)} collective-permute-done((f32[1,112,6144]{2,1,0:T(8,128)S(1)}, f32[1,112,6144]{2,1,0:T(8,128)S(1)}, u32[]{:S(2)}, u32[]{:S(2)}) %collective-permute-start) | collective-permute-done | bytes 2752544 | tf_op jit(solution)/shard_map/ppermute | solution.py:34
  424.3 1.5 copy.114
  (32 shorter events, 2.7 us)
Async XLA Ops:
  0.0 388.0 %copy-start = (f32[1,2,6144]{2,1,0:T(2,128)S(1)}, f32[1,2,6144]{2,1,0:T(2,128)}, u32[]{:S(2)}) copy-start(f32[1,2,6144]{2,1,0:T(2,128)} %param.16) | copy-start | bytes 147460
  0.0 7.6 %copy-start.3 = (bf16[1,112,3,6144]{3,1,2,0:T(8,128)(2,1)S(1)}, bf16[1,112,3,6144]{3,1,2,0:T(8,128)(2,1)}, u32[]{:S(2)}) copy-start(bf16[1,112,3,6144]{3,1,2,0:T(8,128)(2,1)} %param.13) | copy-start | bytes 12386308
  11.0 68.3 %all-to-all-start = ((bf16[8,112,3,768]{3,1,2,0:T(8,128)(2,1)}), bf16[8,112,3,768]{3,1,2,0:T(8,128)(2,1)}, u32[]{:S(2)}, u32[]{:S(2)}) async-start(bf16[8,112,3,768]{3,1,2,0:T(8,128)(2,1)} %fusion.27), calls=%async_computation | async-start | bytes 8257536 | tf_op jit(solution)/shard_map/all_to_all | solution.py:18
  134.0 10.8 %copy-start.1 = (bf16[2,1344,6,128]{3,1,2,0:T(8,128)(2,1)S(1)}, bf16[2,1344,6,128]{3,1,2,0:T(8,128)(2,1)}, u32[]{:S(2)}) copy-start(bf16[2,1344,6,128]{3,1,2,0:T(8,128)(2,1)} %get-tuple-element.270) | copy-start | bytes 12386308 | tf_op jit(solution)/shard_map/while
  144.8 1.3 copy-start.2
  174.5 10.8 %copy-start.1 = (bf16[2,1344,6,128]{3,1,2,0:T(8,128)(2,1)S(1)}, bf16[2,1344,6,128]{3,1,2,0:T(8,128)(2,1)}, u32[]{:S(2)}) copy-start(bf16[2,1344,6,128]{3,1,2,0:T(8,128)(2,1)} %get-tuple-element.270) | copy-start | bytes 12386308 | tf_op jit(solution)/shard_map/while
  185.3 1.3 copy-start.2
  214.3 167.4 %all-to-all-start.1 = ((bf16[8,112,6144]{2,1,0:T(8,128)(2,1)}), bf16[8,112,6144]{2,1,0:T(8,128)(2,1)}, u32[]{:S(2)}, u32[]{:S(2)}) async-start(bf16[8,112,6144]{2,1,0:T(8,128)(2,1)} %bitcast.113), calls=%async_computation.1 | async-start | bytes 22020096 | tf_op jit(solution)/shard_map/all_to_all | solution.py:99
  221.2 166.9 %copy-start.4 = (f32[1,112,6144]{2,1,0:T(8,128)S(1)}, f32[1,112,6144]{2,1,0:T(8,128)}, u32[]{:S(2)}) copy-start(f32[1,112,6144]{2,1,0:T(8,128)} %param.12) | copy-start | bytes 8257540
  389.7 34.7 %collective-permute-start = (f32[1,112,6144]{2,1,0:T(8,128)S(1)}, f32[1,112,6144]{2,1,0:T(8,128)S(1)}, u32[]{:S(2)}, u32[]{:S(2)}) collective-permute-start(f32[1,112,6144]{2,1,0:T(8,128)S(1)} %fusion.26), channel_id=1, source_target_pairs={{0,8},{8,16},{16,24},{24,32},{32,40},{40,48},{48,56},{56,64},{64,7... | collective-permute-start | bytes 8257544 | tf_op jit(solution)/shard_map/ppermute | solution.py:34
